TPU v7x, 256 devices: a whole 4x4x8 slice. The times are simulated.
256 devices in a mesh: gx: 16 (over x, y), gy: 16 (over z, core).
Axes of the slice: x: 4, y: 4, z: 8, core: 2. Of those that a mesh axis runs over, the one named last changes fastest.
Arguments:
- tokens: bfloat16 [2048, 2048], P('gy', 'gx'), may hold values from -6 to 6
- gain: bfloat16 [2048], P('gx'), may hold values from 0.5 to 1.5
- w_router: bfloat16 [2048, 8], P('gx'), may hold values from -0.25 to 0.25
- expert_query_weight: bfloat16 [8, 2048, 16, 128], P(None, 'gx', 'gy'), may hold values from -0.25 to 0.25
- key_value_weight: bfloat16 [2048, 16, 256], P('gx', 'gy'), may hold values from -0.125 to 0.125
- expert_output_weight: bfloat16 [8, 16, 128, 2048], P(None, 'gy', None, 'gx'), may hold values from -0.25 to 0.25
- cache_keys: bfloat16 [16, 16, 4096, 128], P('gx', 'gy'), may hold values from -1220 to 1220
- cached_value_slots: bfloat16 [16, 16, 4096, 128], P('gx', 'gy'), may hold values from -6 to 6
- lengths: int32 [16], replicated, may hold values from 1 to 4096, 34816 in all
- deal: int32 [16], replicated, may hold values from 0 to 15, each once
- route: int32 [2048, 2], replicated, may hold values from 0 to 7, all different within a row
Outputs:
- mixed: bfloat16 [2048, 2048], P('gy', 'gx')
Inputs may be any that keep to these rules, and one draw needn't show every extreme that they name: `lengths`: each request's cache holds between 1 and 4096 keys, and the longest holds exactly 4096. deal[r] is the cache slot of request r; every slot is used once. `route`: each token names 2 different attention experts.
All inputs are finite; a program needn't handle non-finite values.
Results may differ from a plain program's by a relative error of at most 0.01.
The roundings to bfloat16 on the way count: a program that leaves them out, or rounds other values in their place, can miss the bound.
Values may be sent and summed in bfloat16 or wider, within the bound.
No kernel may reach another device: no remote copies, remote signals or barrier semaphores. Data moves between devices by JAX's collectives and lax.ppermute only.
A program may use at most 64 MiB of HBM per device.

v0:
```python
import jax
import jax.numpy as jnp
from jax import lax
from jax.sharding import PartitionSpec as P

masked_score = -1e30
norm_eps = 1e-06


def expert_onehot(route_rows, experts):
    return (route_rows[:, :, None] == jnp.arange(experts, dtype=jnp.int32)[None, None, :]).astype(
        jnp.float32
    )


def absorb(carry_state, scores, value_rows):
    running_max, running_sum, accumulated = carry_state
    new_max = jnp.maximum(running_max, jnp.max(scores, axis=2))
    shrink = jnp.exp(running_max - new_max)
    weights = jnp.exp(scores - new_max[:, :, None])
    running_sum = running_sum * shrink + jnp.sum(weights, axis=2)
    accumulated = accumulated * shrink[:, :, None] + jnp.einsum(
        "hrk,hkd->hrd", weights.astype(jnp.bfloat16), value_rows, preferred_element_type=jnp.float32
    )
    return (new_max, running_sum, accumulated)


def per_device(
    tokens,
    gain,
    w_router,
    expert_query_weight,
    key_value_weight,
    expert_output_weight,
    cache_keys,
    cached_value_slots,
    lengths,
    deal,
    route,
):
    requests = lengths.shape[0]
    experts = expert_query_weight.shape[0]
    heads_local = expert_query_weight.shape[2]
    head_dim = expert_query_weight.shape[3]
    top_count = route.shape[1]
    gathered = lax.all_gather(tokens, "gy", axis=0, tiled=True)
    total_rows, local_width = gathered.shape
    new_len = total_rows // requests
    full_width = local_width * lax.axis_size("gx")
    slot_index = lax.axis_index("gx")
    inverse = jnp.zeros((requests,), jnp.int32).at[deal].set(jnp.arange(requests, dtype=jnp.int32))
    ordered = jnp.take(gathered.reshape(requests, new_len, local_width), inverse, axis=0).reshape(
        total_rows, local_width
    )
    slot_route = jnp.take(route.reshape(requests, new_len, top_count), inverse, axis=0).reshape(
        total_rows, top_count
    )
    widened = ordered.astype(jnp.float32)
    squares = jnp.sum(widened * widened, axis=1)
    scaled_input = (widened * gain.astype(jnp.float32)[None, :]).astype(jnp.bfloat16)
    router_part = jnp.dot(scaled_input, w_router, preferred_element_type=jnp.float32)
    query_part = jnp.einsum(
        "td,edhk->tehk", scaled_input, expert_query_weight, preferred_element_type=jnp.float32
    )
    keyval_part = jnp.einsum(
        "td,dhk->thk", scaled_input, key_value_weight, preferred_element_type=jnp.float32
    )
    my_route = lax.dynamic_slice_in_dim(slot_route, slot_index * new_len, new_len, 0)
    my_onehot = expert_onehot(my_route, experts)
    query_all, keyval_sums, router_sums, square_sums = (
        lax.psum_scatter(query_part, "gx", scatter_dimension=0, tiled=True),
        lax.psum_scatter(keyval_part, "gx", scatter_dimension=0, tiled=True),
        lax.psum_scatter(router_part, "gx", scatter_dimension=0, tiled=True),
        lax.psum_scatter(squares, "gx", scatter_dimension=0, tiled=True),
    )
    query_totals = jnp.sum(my_onehot[:, :, :, None, None] * query_all[:, None], axis=2)
    inverse_root_mean = lax.rsqrt(square_sums / full_width + norm_eps)
    logits = router_sums * inverse_root_mean[:, None]
    chosen = jnp.sum(my_onehot * logits[:, None, :], axis=2)
    gate_gap = chosen[:, 0] - chosen[:, 1]
    gate_weights = jnp.stack([jax.nn.sigmoid(gate_gap), jax.nn.sigmoid(-gate_gap)], axis=1).astype(
        jnp.bfloat16
    )
    query_matrix = (query_totals * inverse_root_mean[:, None, None, None]).astype(jnp.bfloat16)
    key_value_rows = (keyval_sums * inverse_root_mean[:, None, None]).astype(jnp.bfloat16)
    query_rows = new_len * top_count
    query_by_head = jnp.transpose(query_matrix, (2, 0, 1, 3)).reshape(
        heads_local, query_rows, head_dim
    )
    fresh_keyval = jnp.transpose(key_value_rows, (1, 0, 2))
    fresh_keys = fresh_keyval[:, :, :head_dim]
    fresh_values = fresh_keyval[:, :, head_dim:]
    length = jnp.take(lengths, jnp.take(inverse, slot_index))
    local_keys = cache_keys[0]
    local_values = cached_value_slots[0]
    cache_span = local_keys.shape[1]
    key_block = min(1024, cache_span)
    score_scale = head_dim ** (-0.5)
    initial = (
        jnp.full((heads_local, query_rows), masked_score, jnp.float32),
        jnp.zeros((heads_local, query_rows), jnp.float32),
        jnp.zeros((heads_local, query_rows, head_dim), jnp.float32),
    )

    def visit_block(block_index, carry_state):
        first_key = block_index * key_block
        key_rows = lax.dynamic_slice_in_dim(local_keys, first_key, key_block, 1)
        value_rows = lax.dynamic_slice_in_dim(local_values, first_key, key_block, 1)
        scores = (
            jnp.einsum("hrd,hkd->hrk", query_by_head, key_rows, preferred_element_type=jnp.float32)
            * score_scale
        )
        visible = first_key + jnp.arange(key_block, dtype=jnp.int32) < length
        scores = jnp.where(visible[None, None, :], scores, masked_score)
        return absorb(carry_state, scores, value_rows)

    block_count = (length + key_block - 1) // key_block
    carry_state = lax.fori_loop(0, block_count, visit_block, initial)
    fresh_scores = (
        jnp.einsum("hrd,hkd->hrk", query_by_head, fresh_keys, preferred_element_type=jnp.float32)
        * score_scale
    )
    causal = (
        jnp.arange(new_len, dtype=jnp.int32)[None, :]
        <= (jnp.arange(query_rows, dtype=jnp.int32) // top_count)[:, None]
    )
    fresh_scores = jnp.where(causal[None], fresh_scores, masked_score)
    running_max, running_sum, accumulated = absorb(carry_state, fresh_scores, fresh_values)
    attended_output = (accumulated / running_sum[:, :, None]).astype(jnp.bfloat16)
    attended_output = jnp.transpose(
        attended_output.reshape(heads_local, new_len, top_count, head_dim), (1, 2, 0, 3)
    ).reshape(new_len, top_count * heads_local * head_dim)
    all_attended, all_gates = (
        lax.all_gather(attended_output, "gx", axis=0, tiled=True),
        lax.all_gather(gate_weights, "gx", axis=0, tiled=True),
    )
    token_attended = jnp.take(
        all_attended.reshape(requests, new_len, top_count * heads_local * head_dim), deal, axis=0
    ).reshape(total_rows, top_count, heads_local, head_dim)
    token_gates = (
        jnp.take(all_gates.reshape(requests, new_len, top_count), deal, axis=0)
        .reshape(total_rows, top_count)
        .astype(jnp.float32)
    )
    wide_output = expert_output_weight.astype(jnp.float32)
    piece = token_attended.astype(jnp.float32)
    mixing = expert_onehot(route, experts) * token_gates[:, :, None]
    folded = jnp.einsum("tse,tshd->tehd", mixing, piece, precision=lax.Precision.HIGHEST)
    output_sum = lax.psum_scatter(
        jnp.einsum("tehd,ehdo->to", folded, wide_output, precision=lax.Precision.HIGHEST),
        "gy",
        scatter_dimension=0,
        tiled=True,
    )
    return output_sum.astype(jnp.bfloat16)


def solution(mesh):
    placed = (
        P("gy", "gx"),
        P("gx"),
        P("gx", None),
        P(None, "gx", "gy", None),
        P("gx", "gy", None),
        P(None, "gy", None, "gx"),
        P("gx", "gy", None, None),
        P("gx", "gy", None, None),
        P(),
        P(),
        P(),
    )
    return jax.shard_map(
        per_device, mesh=mesh, in_specs=placed, out_specs=P("gy", "gx"), check_vma=False
    )
```

profile of v0, /device:TPU:8, one launch (start us, length us, event | category | flops | bytes accessed | tf_op | source)
XLA Modules:
  0.0 427.1 jit_solution(1710121038791396708)
XLA Ops:
  6.5 0.7 compare_select_fusion.3
  7.2 0.6 scatter_custom_fusion
  7.9 0.7 convert_element_type.98
  8.6 21.6 %all_gather.9 = bf16[2048,128]{1,0:T(8,128)(2,1)S(1)} all-gather(bf16[128,128]{1,0:T(8,128)(2,1)} %param.13), channel_id=1, replica_groups=mesh['gx'=16,'gy'=16] {'gy'}, dimensions={0}, use_global_device_ids=true | all-gather | bytes 557056 | tf_op jit(solution)/shard_map/all_gather | solution.py:46
  30.2 0.6 gather_fusion.1
  31.3 2.6 convolution_bitcast_fusion.2
  34.1 4.5 %convolution_bitcast_fusion.1 = f32[2048,8,1,128]{3,0,1,2:T(8,128)} fusion(bf16[2048,128,1]{1,0,2:T(8,128)(2,1)S(1)} %bitcast.115, bf16[8,128,1,128]{3,1,2,0:T(8,128)(2,1)S(1)} %copy-done), kind=kOutput, calls=%fused_computation.25 | convolution fusion | flops 536870912 | bytes 9175040 | tf_op jit(solution)/shard_map/td,edhk->tehk/dot_general | solution.py:62
  39.0 0.9 fusion.29
  40.0 0.6 dynamic-slice.4
  41.2 0.6 dynamic-slice.5
  42.6 0.6 gather_fusion
  43.3 37.2 %all-reduce = f32[2048]{0:T(1024)S(1)} all-reduce(f32[2048]{0:T(1024)S(1)} %bitcast.128), channel_id=3, replica_groups=mesh['gx'=16,'gy'=16] {'gx'}, use_global_device_ids=true, to_apply=%region_3.4.clone | all-reduce | flops 2048 | bytes 16384
  80.6 0.6 dynamic-slice.6
  82.1 30.0 %reduce-scatter.9.cloned.1.call-done = f32[128,1,256]{2,0,1:T(8,128)} async-done(((f32[2048,1,256]{2,0,1:T(8,128)}), f32[128,1,256]{2,0,1:T(8,128)}) %reduce-scatter.9.cloned.1.call-update) | async-done | bytes 131088 | tf_op jit(solution)/shard_map/reduce_scatter | solution.py:72
  112.1 1.0 fusion.38
  113.1 92.9 %reduce-scatter.7.cloned.1.call-done = f32[128,8,1,128]{3,0,1,2:T(8,128)} async-done(((f32[2048,8,1,128]{3,0,1,2:T(8,128)}), f32[128,8,1,128]{3,0,1,2:T(8,128)}) %reduce-scatter.7.cloned.1.call-update) | async-done | bytes 524304 | tf_op jit(solution)/shard_map/reduce_scatter | solution.py:71
  206.1 1.3 copy.44
  208.2 3.0 while.16
  208.3 1.3 fusion.62
  209.8 1.3 fusion.64
  211.7 0.6 reshape_transpose_reshape.3
  212.9 72.9 %reduce-scatter.5.cloned.1.call-done = f32[128,8]{0,1:T(8,128)} async-done(((f32[2048,8]{0,1:T(8,128)}), f32[128,8]{0,1:T(8,128)}) %reduce-scatter.5.cloned.1.call-update) | async-done | bytes 4112 | tf_op jit(solution)/shard_map/reduce_scatter | solution.py:73
  285.8 0.7 broadcast_multiply_fusion
  286.6 19.8 %all_gather.10 = bf16[2048,2]{0,1:T(2,128)(2,1)S(1)} all-gather(bf16[128,2]{0,1:T(2,128)(2,1)S(1)} %pad_maximum_fusion), channel_id=1, replica_groups=mesh['gx'=16,'gy'=16] {'gx'}, dimensions={0}, use_global_device_ids=true | all-gather | bytes 8704 | tf_op jit(solution)/shard_map/all_gather | solution.py:135
  306.4 0.6 gather_fusion.2
  307.4 27.6 %all-gather.2.cloned.1.call-done = bf16[2048,256]{1,0:T(8,128)(2,1)} async-done(((bf16[128,256]{1,0:T(8,128)(2,1)}), bf16[2048,256]{1,0:T(8,128)(2,1)}) %all-gather.2.cloned.1.call-update) | async-done | bytes 1048592 | tf_op jit(solution)/shard_map/all_gather | solution.py:134
  335.0 1.8 gather_fusion.3
  336.8 1.1 gather.40
  337.9 17.2 %fusion.18 = f32[2048,8,128]{2,1,0:T(8,128)S(1)} fusion(bf16[2048,2,128]{2,1,0:T(2,128)(2,1)} %gather.40, pred[2048]{0:T(1024)(128)(4,1)S(1)} %broadcast_bitcast_fusion.1, f32[2048,2]{1,0:T(8,128)S(1)} %copy.42, s32[2048,2]{1,0:T(8,128)S(1)} %copy.41), kind=kOutput, calls=%fused_computation.29 | convolution fusion | flops 50921472 | bytes 9472000 | tf_op jit(solution)/shard_map/tse,tshd->tehd/dot_general | solution.py:148
  355.2 5.6 %fusion.15 = f32[2048,128]{1,0:T(8,128)} fusion(f32[2048,8,128]{2,1,0:T(8,128)S(1)} %fusion.18, bf16[8,1,128,128]{3,2,1,0:T(8,128)(2,1)S(1)} %copy-done.2), kind=kOutput, calls=%fused_computation.28 | convolution fusion | flops 3221225472 | bytes 9699328 | tf_op jit(solution)/shard_map/tehd,ehdo->to/dot_general | solution.py:150
  360.9 58.2 %reduce-scatter.11.cloned.1.call-done = f32[128,128]{1,0:T(8,128)} async-done(((f32[2048,128]{1,0:T(8,128)}), f32[128,128]{1,0:T(8,128)}) %reduce-scatter.11.cloned.1.call-update) | async-done | bytes 65552 | tf_op jit(solution)/shard_map/reduce_scatter | solution.py:149
  419.1 1.5 convert_element_type.111
  (64 shorter events, 4.0 us)
Async XLA Ops:
  6.5 27.5 %copy-start = (bf16[8,128,1,128]{3,1,2,0:T(8,128)(2,1)S(1)}, bf16[8,128,1,128]{3,1,2,0:T(8,128)(2,1)}, u32[]{:S(2)}) copy-start(bf16[8,128,1,128]{3,1,2,0:T(8,128)(2,1)} %param.16) | copy-start | bytes 786436
  6.5 105.6 %reduce-scatter.9.cloned.1.call-start = ((), (), s32[]{:S(2)}) async-start(), calls=%async_computation.6 | async-start | bytes 2228224 | tf_op jit(solution)/shard_map/reduce_scatter | solution.py:72
  34.0 172.1 %reduce-scatter.7.cloned.1.call-start = ((), (), s32[]{:S(2)}) async-start(), calls=%async_computation.5 | async-start | bytes 8912896 | tf_op jit(solution)/shard_map/reduce_scatter | solution.py:71
  34.0 5.0 %copy-start.3 = (bf16[128,8]{0,1:T(8,128)(2,1)S(1)}, bf16[128,8]{0,1:T(8,128)(2,1)}, u32[]{:S(2)}) copy-start(bf16[128,8]{0,1:T(8,128)(2,1)} %param.15) | copy-start | bytes 6148
  34.0 7.2 %copy-start.4 = (s32[16]{0:T(128)S(1)}, s32[16]{0:T(128)}, u32[]{:S(2)}) copy-start(s32[16]{0:T(128)} %param.21) | copy-start | bytes 196
  34.0 8.5 %copy-start.1 = (s32[2048,2]{0,1:T(2,128)S(1)}, s32[2048,2]{0,1:T(2,128)}, u32[]{:S(2)}) copy-start(s32[2048,2]{0,1:T(2,128)} %param.23) | copy-start | bytes 49156
  38.5 42.1 %copy-start.6 = (u32[256]{0:T(256)S(1)}, u32[256]{0:T(256)}, u32[]{:S(2)}) copy-start(u32[256]{0:T(256)} %constant.201) | copy-start | bytes 3076
  38.5 247.3 %reduce-scatter.5.cloned.1.call-start = ((), (), s32[]{:S(2)}) async-start(), calls=%async_computation.4 | async-start | bytes 69632 | tf_op jit(solution)/shard_map/reduce_scatter | solution.py:73
  39.9 295.0 %all-gather.2.cloned.1.call-start = ((), (), s32[]{:S(2)}) async-start(), calls=%async_computation.7 | async-start | bytes 1114112 | tf_op jit(solution)/shard_map/all_gather | solution.py:134
  208.2 4.6 %copy-start.5 = (s32[16]{0:T(128)S(1)}, s32[16]{0:T(128)}, u32[]{:S(2)}) copy-start(s32[16]{0:T(128)} %param.22) | copy-start | bytes 196
  212.3 206.7 %reduce-scatter.11.cloned.1.call-start = ((), (), s32[]{:S(2)}) async-start(), calls=%async_computation.8 | async-start | bytes 1114112 | tf_op jit(solution)/shard_map/reduce_scatter | solution.py:149
  337.9 17.2 %copy-start.2 = (bf16[8,1,128,128]{3,2,1,0:T(8,128)(2,1)S(1)}, bf16[8,1,128,128]{3,2,1,0:T(8,128)(2,1)}, u32[]{:S(2)}) copy-start(bf16[8,1,128,128]{3,2,1,0:T(8,128)(2,1)} %param.18) | copy-start | bytes 786436
Sparse Core Ops, SparseCore 0:
  34.1 78.0 reduce-scatter.8
  115.8 90.2 reduce-scatter.6
  209.5 76.2 reduce-scatter.4
  288.1 46.8 all-gather.1
  361.0 58.0 reduce-scatter.10
where the time goes:
time: 428 us; the launch traced here: 427 us
  waiting for transfers between devices  282 us (66%)
  blocking collectives  78.7 us (18%)
  matrix products  33.9 us (8%)
  between operations  15.4 us (4%)
  local copies, waits for them, and re-layouts  10.6 us (2%)
  other arithmetic  6.49 us (2%)
    reduce_scatter x1, waiting for transfers between devices, per_device(): lax.psum_scatter(query_part, 'gx', scatter_dimension=0, tiled=True)  92.9 us
    reduce_scatter x1, waiting for transfers between devices, per_device(): lax.psum_scatter(router_part, 'gx', scatter_dimension=0, tiled=True)  72.9 us
    reduce_scatter x1, waiting for transfers between devices, per_device(): lax.psum_scatter(jnp.einsum('tehd,ehdo->to', folded, wide_output, precisi...  58.2 us
    unnamed x1, blocking collectives  37.2 us
    reduce_scatter x1, waiting for transfers between devices, per_device(): lax.psum_scatter(keyval_part, 'gx', scatter_dimension=0, tiled=True)  30 us
    all_gather x1, waiting for transfers between devices, per_device(): lax.all_gather(attended_output, 'gx', axis=0, tiled=True)  27.6 us
    all_gather x1, blocking collectives, per_device(): gathered = lax.all_gather(tokens, 'gy', axis=0, tiled=True)  21.6 us
    all_gather x1, blocking collectives, per_device(): lax.all_gather(gate_weights, 'gx', axis=0, tiled=True)  19.8 us
  transfers between devices with their start and end apart: 5, of which 5 were waited for; matrix products, arithmetic and copies ran while one was open for 4% of the time, Pallas kernels for 0%

commit v1 on v0

--- a/solution.py
+++ b/solution.py
@@ -2,9 +2,14 @@
 import jax.numpy as jnp
 from jax import lax
 from jax.sharding import PartitionSpec as P
+from jax.lax import all_to_all, axis_size
 
 masked_score = -1e30
 norm_eps = 1e-06
+things_mix = lambda here_x: jnp.concatenate(
+    all_to_all(jnp.stack(axis_size("gx") * [here_x]), axis_name="gx", split_axis=0, concat_axis=0),
+    axis=0,
+)
 
 
 def expert_onehot(route_rows, experts):
@@ -131,7 +136,7 @@
         attended_output.reshape(heads_local, new_len, top_count, head_dim), (1, 2, 0, 3)
     ).reshape(new_len, top_count * heads_local * head_dim)
     all_attended, all_gates = (
-        lax.all_gather(attended_output, "gx", axis=0, tiled=True),
+        things_mix(attended_output),
         lax.all_gather(gate_weights, "gx", axis=0, tiled=True),
     )
     token_attended = jnp.take(

time: 428 us -> 406 us (0.949)
  waiting for transfers between devices: 282 us -> 246 us
  starting transfers between devices: 0.17 us -> 14.4 us
    all_gather x1 -> x0, waiting for transfers between devices: 27.6 us -> none  [per_device(): lax.all_gather(attended_output, 'gx', axis=0, tiled=True)]
    all_to_all x0 -> x1, starting transfers between devices: none -> 14.3 us  [all_to_all(jnp.stack(axis_size('gx') * [here_x]), axis_name='gx', split_a...]
    reduce_scatter x1, waiting for transfers between devices: 72.9 us -> 64.1 us  [per_device(): lax.psum_scatter(router_part, 'gx', scatter_dimension=0, tiled=True)]
  transfers between devices with their start and end apart: 5 -> 5, of which waited for: 5 -> 4; matrix products, arithmetic and copies ran while one was open for 4% -> 5% of each run, Pallas kernels for 0% -> 0%
where the time goes in v1:
time: 406 us; the launch traced here: 405 us
  waiting for transfers between devices  246 us (61%)
  blocking collectives  78.4 us (19%)
  matrix products  34 us (8%)
  between operations  15.4 us (4%)
  starting transfers between devices  14.4 us (4%)
  local copies, waits for them, and re-layouts  10.3 us (3%)
  other arithmetic  6.51 us (2%)
    reduce_scatter x1, waiting for transfers between devices, per_device(): lax.psum_scatter(query_part, 'gx', scatter_dimension=0, tiled=True)  93.3 us
    reduce_scatter x1, waiting for transfers between devices, per_device(): lax.psum_scatter(router_part, 'gx', scatter_dimension=0, tiled=True)  64.1 us
    reduce_scatter x1, waiting for transfers between devices, per_device(): lax.psum_scatter(jnp.einsum('tehd,ehdo->to', folded, wide_output, precisi...  58.7 us
    unnamed x1, blocking collectives  37.1 us
    reduce_scatter x1, waiting for transfers between devices, per_device(): lax.psum_scatter(keyval_part, 'gx', scatter_dimension=0, tiled=True)  29.5 us
    all_gather x1, blocking collectives, per_device(): gathered = lax.all_gather(tokens, 'gy', axis=0, tiled=True)  21.6 us
    all_gather x1, blocking collectives, per_device(): lax.all_gather(gate_weights, 'gx', axis=0, tiled=True)  19.6 us
    dot_general x1, matrix products, per_device(): jnp.einsum('tse,tshd->tehd', mixing, piece, precision=lax.Precision.HIGHEST)  17.3 us
  transfers between devices with their start and end apart: 5, of which 4 were waited for; matrix products, arithmetic and copies ran while one was open for 5% of the time, Pallas kernels for 0%

profile of v1, /device:TPU:8, one launch (start us, length us, event | category | flops | bytes accessed | tf_op | source)
XLA Modules:
  0.0 404.7 jit_solution(5366508733099869309)
XLA Ops:
  6.5 0.7 compare_select_fusion.3
  7.2 0.6 scatter_custom_fusion
  7.9 0.7 convert_element_type.98
  8.6 21.6 %all_gather.6 = bf16[2048,128]{1,0:T(8,128)(2,1)S(1)} all-gather(bf16[128,128]{1,0:T(8,128)(2,1)} %param.13), channel_id=1, replica_groups=mesh['gx'=16,'gy'=16] {'gy'}, dimensions={0}, use_global_device_ids=true | all-gather | bytes 557056 | tf_op jit(solution)/shard_map/all_gather | solution.py:51
  30.2 0.6 gather_fusion.1
  31.3 2.7 convolution_bitcast_fusion.2
  34.1 4.5 %convolution_bitcast_fusion.1 = f32[2048,8,1,128]{3,0,1,2:T(8,128)} fusion(bf16[2048,128,1]{1,0,2:T(8,128)(2,1)S(1)} %bitcast.114, bf16[8,128,1,128]{3,1,2,0:T(8,128)(2,1)S(1)} %copy-done), kind=kOutput, calls=%fused_computation.25 | convolution fusion | flops 536870912 | bytes 9175040 | tf_op jit(solution)/shard_map/td,edhk->tehk/dot_general | solution.py:67
  39.1 0.9 fusion.29
  40.0 0.6 dynamic-slice.4
  41.3 0.6 dynamic-slice.5
  43.1 0.6 gather_fusion
  43.8 37.1 %all-reduce = f32[2048]{0:T(1024)S(1)} all-reduce(f32[2048]{0:T(1024)S(1)} %bitcast.126), channel_id=3, replica_groups=mesh['gx'=16,'gy'=16] {'gx'}, use_global_device_ids=true, to_apply=%region_3.4.clone | all-reduce | flops 2048 | bytes 16384
  81.0 0.6 dynamic-slice.6
  82.5 29.5 %reduce-scatter.9.cloned.1.call-done = f32[128,1,256]{2,0,1:T(8,128)} async-done(((f32[2048,1,256]{2,0,1:T(8,128)}), f32[128,1,256]{2,0,1:T(8,128)}) %reduce-scatter.9.cloned.1.call-update) | async-done | bytes 131088 | tf_op jit(solution)/shard_map/reduce_scatter | solution.py:77
  112.1 1.0 fusion.38
  113.1 93.3 %reduce-scatter.7.cloned.1.call-done = f32[128,8,1,128]{3,0,1,2:T(8,128)} async-done(((f32[2048,8,1,128]{3,0,1,2:T(8,128)}), f32[128,8,1,128]{3,0,1,2:T(8,128)}) %reduce-scatter.7.cloned.1.call-update) | async-done | bytes 524304 | tf_op jit(solution)/shard_map/reduce_scatter | solution.py:76
  206.4 1.3 copy.44
  208.5 3.0 while.16
  208.5 1.3 fusion.62
  210.1 1.3 fusion.64
  212.0 1.1 stack.10
  213.1 14.3 %all-to-all-start = ((bf16[16,128,256]{2,1,0:T(8,128)(2,1)}), bf16[16,128,256]{2,1,0:T(8,128)(2,1)S(1)}, u32[]{:S(2)}, u32[]{:S(2)}) async-start(bf16[16,128,256]{2,1,0:T(8,128)(2,1)} %stack.10), calls=%async_computation.3 | async-start | bytes 2097152 | tf_op jit(solution)/shard_map/all_to_all | solution.py:10
  227.4 64.1 %reduce-scatter.5.cloned.1.call-done = f32[128,8]{0,1:T(8,128)} async-done(((f32[2048,8]{0,1:T(8,128)}), f32[128,8]{0,1:T(8,128)}) %reduce-scatter.5.cloned.1.call-update) | async-done | bytes 4112 | tf_op jit(solution)/shard_map/reduce_scatter | solution.py:78
  291.5 0.7 broadcast_multiply_fusion
  292.3 19.6 %all_gather.7 = bf16[2048,2]{0,1:T(2,128)(2,1)S(1)} all-gather(bf16[128,2]{0,1:T(2,128)(2,1)S(1)} %pad_maximum_fusion), channel_id=1, replica_groups=mesh['gx'=16,'gy'=16] {'gx'}, dimensions={0}, use_global_device_ids=true | all-gather | bytes 8704 | tf_op jit(solution)/shard_map/all_gather | solution.py:140
  311.9 0.6 gather_fusion.2
  312.5 1.4 copy.42
  313.9 0.6 gather_fusion.3
  315.1 17.3 %fusion.18 = f32[2048,8,128]{2,1,0:T(8,128)S(1)} fusion(bf16[2048,2,128]{2,1,0:T(2,128)(2,1)S(1)} %gather.40, pred[2048]{0:T(1024)(128)(4,1)S(1)} %broadcast_bitcast_fusion.1, f32[2048,2]{1,0:T(8,128)} %copy.42, s32[2048,2]{1,0:T(8,128)S(1)} %copy.41), kind=kOutput, calls=%fused_computation.29 | convolution fusion | flops 50921472 | bytes 9472000 | tf_op jit(solution)/shard_map/tse,tshd->tehd/dot_general | solution.py:153
  332.3 5.6 %fusion.15 = f32[2048,128]{1,0:T(8,128)} fusion(f32[2048,8,128]{2,1,0:T(8,128)S(1)} %fusion.18, bf16[8,1,128,128]{3,2,1,0:T(8,128)(2,1)S(1)} %copy-done.2), kind=kOutput, calls=%fused_computation.28 | convolution fusion | flops 3221225472 | bytes 9699328 | tf_op jit(solution)/shard_map/tehd,ehdo->to/dot_general | solution.py:155
  338.0 58.7 %reduce-scatter.11.cloned.1.call-done = f32[128,128]{1,0:T(8,128)} async-done(((f32[2048,128]{1,0:T(8,128)}), f32[128,128]{1,0:T(8,128)}) %reduce-scatter.11.cloned.1.call-update) | async-done | bytes 65552 | tf_op jit(solution)/shard_map/reduce_scatter | solution.py:154
  396.7 1.5 convert_element_type.111
  (64 shorter events, 4.1 us)
Async XLA Ops:
  6.5 27.5 %copy-start = (bf16[8,128,1,128]{3,1,2,0:T(8,128)(2,1)S(1)}, bf16[8,128,1,128]{3,1,2,0:T(8,128)(2,1)}, u32[]{:S(2)}) copy-start(bf16[8,128,1,128]{3,1,2,0:T(8,128)(2,1)} %param.16) | copy-start | bytes 786436
  6.5 105.5 %reduce-scatter.9.cloned.1.call-start = ((), (), s32[]{:S(2)}) async-start(), calls=%async_computation.7 | async-start | bytes 2228224 | tf_op jit(solution)/shard_map/reduce_scatter | solution.py:77
  34.0 172.4 %reduce-scatter.7.cloned.1.call-start = ((), (), s32[]{:S(2)}) async-start(), calls=%async_computation.6 | async-start | bytes 8912896 | tf_op jit(solution)/shard_map/reduce_scatter | solution.py:76
  34.0 5.0 %copy-start.3 = (bf16[128,8]{0,1:T(8,128)(2,1)S(1)}, bf16[128,8]{0,1:T(8,128)(2,1)}, u32[]{:S(2)}) copy-start(bf16[128,8]{0,1:T(8,128)(2,1)} %param.15) | copy-start | bytes 6148
  34.0 5.9 %copy-start.4 = (s32[16]{0:T(128)S(1)}, s32[16]{0:T(128)}, u32[]{:S(2)}) copy-start(s32[16]{0:T(128)} %param.22) | copy-start | bytes 196
  34.1 7.2 %copy-start.5 = (s32[16]{0:T(128)S(1)}, s32[16]{0:T(128)}, u32[]{:S(2)}) copy-start(s32[16]{0:T(128)} %param.21) | copy-start | bytes 196
  34.1 8.6 %copy-start.1 = (s32[2048,2]{0,1:T(2,128)S(1)}, s32[2048,2]{0,1:T(2,128)}, u32[]{:S(2)}) copy-start(s32[2048,2]{0,1:T(2,128)} %param.23) | copy-start | bytes 49156
  38.5 42.4 %copy-start.6 = (u32[256]{0:T(256)S(1)}, u32[256]{0:T(256)}, u32[]{:S(2)}) copy-start(u32[256]{0:T(256)} %constant.201) | copy-start | bytes 3076
  38.6 253.0 %reduce-scatter.5.cloned.1.call-start = ((), (), s32[]{:S(2)}) async-start(), calls=%async_computation.5 | async-start | bytes 69632 | tf_op jit(solution)/shard_map/reduce_scatter | solution.py:78
  213.1 100.9 %all-to-all-start = ((bf16[16,128,256]{2,1,0:T(8,128)(2,1)}), bf16[16,128,256]{2,1,0:T(8,128)(2,1)S(1)}, u32[]{:S(2)}, u32[]{:S(2)}) async-start(bf16[16,128,256]{2,1,0:T(8,128)(2,1)} %stack.10), calls=%async_computation.3 | async-start | bytes 2097152 | tf_op jit(solution)/shard_map/all_to_all | solution.py:10
  227.4 169.3 %reduce-scatter.11.cloned.1.call-start = ((), (), s32[]{:S(2)}) async-start(), calls=%async_computation.8 | async-start | bytes 1114112 | tf_op jit(solution)/shard_map/reduce_scatter | solution.py:154
  315.0 17.3 %copy-start.2 = (bf16[8,1,128,128]{3,2,1,0:T(8,128)(2,1)S(1)}, bf16[8,1,128,128]{3,2,1,0:T(8,128)(2,1)}, u32[]{:S(2)}) copy-start(bf16[8,1,128,128]{3,2,1,0:T(8,128)(2,1)} %param.18) | copy-start | bytes 786436
Sparse Core Ops, SparseCore 0:
  34.1 77.9 reduce-scatter.8
  115.8 90.5 reduce-scatter.6
  209.8 81.6 reduce-scatter.4
  338.1 58.5 reduce-scatter.10
